TPU v7x, 128 devices: a whole 4x4x4 slice. The times are simulated.
128 devices in a mesh: gx: 4 (over x_lo, core), gy: 8 (over y, x_hi), gz: 4 (over z).
Axes of the slice: x: 4 (x_hi: 2, x_lo: 2; x = x_hi * 2 + x_lo), y: 4, z: 4, core: 2. Of those that a mesh axis runs over, the one named last changes fastest.
Arguments:
- state: float32 [4, 96, 128, 2048], P(None, 'gz', 'gx', 'gy'), may hold values from -5 to 5
- mixing: float32 [2, 96, 128, 2048], P(None, 'gz', 'gx', 'gy'), may hold values from 0.1 to 1000
- depth_levels: int32 [128, 2048], replicated, may hold values from 0 to 96
- wind: float32 [2, 128, 2048], P(None, 'gx', 'gy'), may hold values from -3 to 3
Outputs:
- state_next: float32 [4, 96, 128, 2048], P(None, 'gz', 'gx', 'gy')
Inputs may be any that keep to these rules, and one draw needn't show every extreme that they name: `depth_levels`: levels at or beyond a column's count are land.
All inputs are finite; a program needn't handle non-finite values.
Results may differ from a plain program's by a relative error of at most 0.0003.
Values sent between devices are 32-bit elements; how exact they have to be, the bound alone decides.
No kernel may reach another device: no remote copies, remote signals or barrier semaphores. Data moves between devices by JAX's collectives and lax.ppermute only.
A program may use at most 192 MiB of HBM per device.

v0:
```python
import jax
import jax.numpy as jnp
from jax import lax
from jax.sharding import PartitionSpec as P


def padded_2(array, sides, width):
    for axis, dim in sides:
        peers, length = (lax.axis_size(axis), array.shape[dim])
        up = [(i, (i + 1) % peers) for i in range(peers)]
        down = [(j, i) for i, j in up]
        last = lax.slice_in_dim(array, length - width, length, axis=dim)
        initial = lax.slice_in_dim(array, 0, width, axis=dim)
        before = lax.ppermute(last, axis, up)
        after = lax.ppermute(initial, axis, down)
        array = jnp.concatenate([before, array, after], axis=dim)
    return array


def carried_in(part, axis, combine, identity):
    place = lax.axis_index(axis)
    gathered = lax.all_gather(part, axis)
    state = jnp.zeros_like(part) + jnp.asarray(identity, part.dtype)

    def one(turn, state):
        return combine(state, lax.dynamic_index_in_dim(gathered, turn, 0, False))

    return lax.fori_loop(0, place, one, state)


def density_of(fields, wet_mask):
    return (-0.3 * fields[0] + 0.7 * fields[1] - 0.05 * fields[0] * fields[0]) * wet_mask


def advance(padded, wet_pad, pressure, wall_face, coriolis):
    wet_x = wet_pad[:, :-1, 1:-1] * wet_pad[:, 1:, 1:-1]
    wet_y = wet_pad[:, 1:-1, :-1] * wet_pad[:, 1:-1, 1:] * wall_face
    east_vel = 0.5 * (padded[2, :, :-1, 1:-1] + padded[2, :, 1:, 1:-1]) * wet_x
    north_vel = 0.5 * (padded[3, :, 1:-1, :-1] + padded[3, :, 1:-1, 1:]) * wet_y
    west_side = padded[:, :, :-1, 1:-1]
    east_side = padded[:, :, 1:, 1:-1]
    flux_x = 0.25 * (
        jnp.maximum(east_vel, 0.0) * west_side + jnp.minimum(east_vel, 0.0) * east_side
    ) - 0.08 * wet_x * (east_side - west_side)
    south_side = padded[:, :, 1:-1, :-1]
    north_side = padded[:, :, 1:-1, 1:]
    flux_y = 0.25 * (
        jnp.maximum(north_vel, 0.0) * south_side + jnp.minimum(north_vel, 0.0) * north_side
    ) - 0.08 * wet_y * (north_side - south_side)
    interior = padded[:, :, 1:-1, 1:-1]
    moved = interior - (
        flux_x[:, :, 1:] - flux_x[:, :, :-1] + flux_y[:, :, :, 1:] - flux_y[:, :, :, :-1]
    )
    centre = pressure[:, 1:-1, 1:-1]
    grad_x = 0.5 * (
        wet_x[:, 1:] * (pressure[:, 2:, 1:-1] - centre)
        + wet_x[:, :-1] * (centre - pressure[:, :-2, 1:-1])
    )
    grad_y = 0.5 * (
        wet_y[:, :, 1:] * (pressure[:, 1:-1, 2:] - centre)
        + wet_y[:, :, :-1] * (centre - pressure[:, 1:-1, :-2])
    )
    east_new = moved[2] + 0.3 * coriolis * interior[3] - grad_x
    north_new = moved[3] - 0.3 * coriolis * interior[2] - grad_y
    wet_inner = wet_pad[:, 1:-1, 1:-1]
    return jnp.stack([moved[0], moved[1], east_new, north_new]) * wet_inner


def thomas(rhs_lev, below_lev, above_lev):

    def forward(carry, item):
        ratio_prev, value_prev = carry
        rhs_here, below_here, above_here = item
        divisor = 1.0 + above_here * (1.0 - ratio_prev) + below_here
        ratio = below_here / divisor
        value = (rhs_here + above_here * value_prev) / divisor
        return ((ratio, value), (ratio, value))

    zero_level = jnp.zeros_like(rhs_lev[0])
    ratio_start = jnp.zeros_like(below_lev[0] * rhs_lev[0])
    _, (ratios, values) = lax.scan(
        forward, (ratio_start, zero_level), (rhs_lev, below_lev, above_lev), unroll=8
    )

    def backward(later, item):
        ratio, value = item
        result = value + ratio * later
        return (result, result)

    _, solved = lax.scan(backward, zero_level, (ratios, values), reverse=True, unroll=8)
    return solved


def tridiagonal(forced, coupling):
    below = jnp.repeat(coupling, 2, axis=0)
    above = jnp.concatenate([jnp.zeros_like(below[:, :1]), below[:, :-1]], axis=1)
    solved = thomas(
        jnp.moveaxis(forced, 1, 0), jnp.moveaxis(below, 1, 0), jnp.moveaxis(above, 1, 0)
    )
    return jnp.moveaxis(solved, 0, 1)


def add_totals(earlier, later):
    return earlier + later


def per_device(state, mixing, depth_levels, wind):
    fields, lev_count, col_x, col_y = state.shape
    total_x, total_y = depth_levels.shape
    start_x = lax.axis_index("gx") * col_x
    start_y = lax.axis_index("gy") * col_y
    start_z = lax.axis_index("gz") * lev_count
    padded = padded_2(state, (("gx", 2), ("gy", 3)), 1)
    row_index = (start_x - 1 + jnp.arange(col_x + 2, dtype=jnp.int32)) % total_x
    col_index = (start_y - 1 + jnp.arange(col_y + 2, dtype=jnp.int32)) % total_y
    depth_pad = jnp.take(jnp.take(depth_levels, row_index, axis=0), col_index, axis=1)
    levels = start_z + jnp.arange(lev_count, dtype=jnp.int32)
    wet_pad = (levels[:, None, None] < depth_pad[None]).astype(jnp.float32)
    density_field = density_of(padded, wet_pad)
    inclusive = jnp.cumsum(density_field, axis=0)
    column_total = inclusive[-1]
    shallower = carried_in(column_total, "gz", add_totals, jnp.zeros_like(column_total))
    pressure = 0.03 * (shallower[None] + inclusive - 0.5 * density_field)
    face_row = start_y - 1 + jnp.arange(col_y + 1, dtype=jnp.int32)
    wall_face = ((face_row >= 0) & (face_row <= total_y - 2)).astype(jnp.float32)
    row_global = start_y + jnp.arange(col_y, dtype=jnp.int32)
    coriolis = 0.5 + (row_global.astype(jnp.float32) + 0.5) / total_y
    forced = advance(padded, wet_pad, pressure, wall_face, coriolis)
    wet_inner = wet_pad[:, 1:-1, 1:-1]
    depth_inner = depth_pad[1:-1, 1:-1]
    wet_next = ((levels + 1)[:, None, None] < depth_inner[None]).astype(jnp.float32)
    top_level = (levels == 0).astype(jnp.float32)
    forced = forced.at[2:].add(wind[:, None] * top_level[None, :, None, None] * wet_inner[None])
    coupling = mixing * (wet_inner * wet_next)[None]
    whole_forced, whole_coupling = (
        lax.all_gather(forced, "gz", axis=1, tiled=True),
        lax.all_gather(coupling, "gz", axis=1, tiled=True),
    )
    solved = tridiagonal(whole_forced, whole_coupling)
    result = lax.dynamic_slice_in_dim(solved, start_z, lev_count, 1)
    return result


def solution(mesh):
    return jax.shard_map(
        per_device,
        mesh=mesh,
        in_specs=(P(None, "gz", "gx", "gy"), P(None, "gz", "gx", "gy"), P(), P(None, "gx", "gy")),
        out_specs=P(None, "gz", "gx", "gy"),
        check_vma=False,
    )
```

profile of v0, /device:TPU:1, one launch (start us, length us, event | category | flops | bytes accessed | tf_op | source)
XLA Modules:
  0.0 404.7 jit_solution(3733420670964093776)
XLA Ops:
  13.1 2.9 broadcast_multiply_fusion
  16.9 2.6 collective-permute-start
  20.1 1.9 constant_dynamic-update-slice_fusion
  24.2 2.6 fusion.103
  26.8 2.4 copy.21
  29.2 2.4 collective-permute-start.2
  31.6 2.5 copy.23
  34.1 3.0 collective-permute-start.3
  37.1 2.8 dynamic-update-slice.28
  39.9 2.8 broadcast_maximum_fusion.1
  45.2 2.9 multiply_subtract_fusion.1
  48.1 2.1 copy.22
  50.3 2.9 copy.24
  53.1 3.1 compare_select_fusion
  56.3 5.1 %fusion.106 = f32[24,34,258]{2,1,0:T(8,128)S(1)} fusion(f32[24,34,258]{2,1,0:T(8,128)S(1)} %compare_select_fusion), kind=kOutput, calls=%fused_computation.238 | output fusion | flops 4842144 | bytes 1684224 | tf_op jit(solution)/shard_map/jit(cumsum)/reduce_window_sum | solution.py:120
  63.5 2.9 multiply_subtract_fusion
  66.4 3.1 fusion.43
  70.3 13.5 %all_gather.10 = f32[4,34,258]{2,1,0:T(8,128)S(1)} all-gather(f32[1,34,258]{2,1,0:T(8,128)S(1)} %slice-done.1), channel_id=1, replica_groups=mesh['gx'=4,'gy'=8,'gz'=4] {'gz'}, dimensions={0}, use_global_device_ids=true | all-gather | bytes 175440 | tf_op jit(solution)/shard_map/all_gather | solution.py:22
  83.9 2.2 subtract_multiply_fusion
  86.3 2.6 fusion.69
  91.9 3.9 copy.20
  95.8 7.3 %broadcast_in_dim.186 = f32[2,2,96,32,256]{4,3,1,0,2:T(8,128)} broadcast(f32[2,96,32,256]{3,2,0,1:T(8,128)S(1)} %copy.20), dimensions={0,2,3,4} | broadcast | bytes 18874368 | tf_op jit(solution)/shard_map/broadcast_in_dim | solution.py:95
  103.2 13.2 %slice.499 = f32[4,95,32,256]{3,2,0,1:T(8,128)} slice(f32[4,96,32,256]{3,2,0,1:T(8,128)} %bitcast.484), slice={[0:4], [0:95], [0:32], [0:256]} | slice | bytes 24903680 | tf_op jit(solution)/shard_map/slice | solution.py:96
  116.3 12.0 %concatenate.42 = f32[4,96,32,256]{3,2,0,1:T(8,128)} pad(f32[4,95,32,256]{3,2,0,1:T(8,128)} %slice.499, f32[]{:T(128)} %constant.186.clone.1), padding=0_0x1_0x0_0x0_0 | pad | bytes 25034756 | tf_op jit(solution)/shard_map/concatenate | solution.py:96
  128.3 82.5 %all-gather.5.cloned.1.call-done = f32[4,96,32,256]{3,2,1,0:T(8,128)} async-done(((f32[4,24,32,256]{3,2,1,0:T(8,128)}), f32[4,96,32,256]{3,2,1,0:T(8,128)}) %all-gather.5.cloned.1.call-update) | async-done | bytes 12582928 | tf_op jit(solution)/shard_map/all_gather | solution.py:136
  210.8 141.2 %while.46 = (s32[]{:T(128)}, f32[4,32,256]{2,1,0:T(8,128)S(1)}, f32[4,32,256]{2,1,0:T(8,128)S(1)}, f32[12,8,4,32,256]{4,3,2,1,0:T(8,128)}, f32[12,8,4,32,256]{4,...) while((s32[]{:T(128)}, f32[4,32,256]{2,1,0:T(8,128)S(1)}, ...), condition=%wide.region_4.5_spmd.clone, body=%wide.region_3.4_spmd.clone.sunk | while | flops 2162696 | bytes 14943063 | solution.py:81
  352.0 6.2 %broadcast.313.clone = f32[12,8,4,32,256]{4,3,1,0,2:T(8,128)} broadcast(f32[]{:T(128)} %constant.186.clone.1), dimensions={} | broadcast | bytes 12582916 | tf_op jit(solution)/shard_map/broadcast.15
  358.1 35.6 %while.47 = (s32[]{:T(128)}, f32[4,32,256]{2,1,0:T(8,128)S(1)}, f32[12,8,4,32,256]{4,3,1,0,2:T(8,128)}, f32[12,8,4,32,256]{4,3,2,1,0:T(8,128)}, f32[12,8,4,32,25...) while((s32[]{:T(128)}, f32[4,32,256]{2,1,0:T(8,128)S(1)}, ...), condition=%wide.region_6.7_spmd.clone, body=%wide.region_5.6_spmd.clone.sunk | while | flops 557066 | bytes 7340315 | solution.py:90
  358.1 1.8 bitcast_dynamic-update-slice_fusion.54
  361.1 1.8 bitcast_dynamic-update-slice_fusion.54
  364.1 1.8 bitcast_dynamic-update-slice_fusion.54
  393.8 4.1 %dynamic-slice_bitcast_fusion.40 = f32[4,24,32,256]{3,2,1,0:T(8,128)} fusion(f32[96,4,32,256]{3,2,0,1:T(8,128)} %bitcast.487, s32[]{:T(128)S(6)} %select_n.96), kind=kLoop, calls=%fused_computation.139 | loop fusion | bytes 6291460 | tf_op jit(solution)/shard_map/dynamic_slice | solution.py:140
  (318 shorter events, 188.9 us)
Async XLA Ops:
  6.5 1.2 copy-start
  6.5 85.4 %all-gather.3.cloned.1.call-start = ((), (), s32[]{:S(2)}) async-start(), calls=%async_computation | async-start | bytes 7864320 | tf_op jit(solution)/shard_map/all_gather | solution.py:137
  10.3 0.5 copy-start.18
  10.8 1.1 copy-start.5
  13.1 3.0 copy-start.2
  16.1 194.8 %all-gather.5.cloned.1.call-start = ((), (), s32[]{:S(2)}) async-start(), calls=%async_computation.1 | async-start | bytes 15728640 | tf_op jit(solution)/shard_map/all_gather | solution.py:136
  16.9 5.6 %collective-permute-start = (f32[4,24,1,256]{3,2,1,0:T(1,128)}, f32[4,24,1,256]{3,2,1,0:T(1,128)S(1)}, u32[]{:S(2)}, u32[]{:S(2)}) collective-permute-start(f32[4,24,1,256]{3,2,1,0:T(1,128)} %get-tuple-element.347), channel_id=1, source_target_pairs={{0,32},{32,64},{64,96},{96,0},{1,33},{33,65},{65,97},{97,1},{2,34}... | collective-permute-start | bytes 294920 | tf_op jit(solution)/shard_map/ppermute | solution.py:14
  19.5 4.0 collective-permute-start.1
  29.2 19.0 %collective-permute-start.2 = (f32[4,24,34,1]{2,1,3,0:T(8,128)S(1)}, f32[4,24,34,1]{2,1,3,0:T(8,128)S(1)}, u32[]{:S(2)}, u32[]{:S(2)}) collective-permute-start(f32[4,24,34,1]{2,1,3,0:T(8,128)S(1)} %copy.21), channel_id=1, source_target_pairs={{0,4},{4,8},{8,12},{12,16},{16,20},{20,24},{24,28},{28,0},{1,5},{5... | collective-permute-start | bytes 39176 | tf_op jit(solution)/shard_map/ppermute | solution.py:14
  34.1 16.2 %collective-permute-start.3 = (f32[4,24,34,1]{2,1,3,0:T(8,128)S(1)}, f32[4,24,34,1]{2,1,3,0:T(8,128)}, u32[]{:S(2)}, u32[]{:S(2)}) collective-permute-start(f32[4,24,34,1]{2,1,3,0:T(8,128)S(1)} %copy.23), channel_id=1, source_target_pairs={{4,0},{8,4},{12,8},{16,12},{20,16},{24,20},{28,24},{0,28},{5,1},{9... | collective-permute-start | bytes 39176 | tf_op jit(solution)/shard_map/ppermute | solution.py:15
  42.7 1.0 copy-start.13
  42.7 2.5 copy-start.9
  48.1 5.0 %copy-start.19 = (s32[24]{0:T(128)S(1)}, s32[24]{0:T(128)}, u32[]{:S(2)}) copy-start(s32[24]{0:T(128)} %copy-done.18) | copy-start | bytes 292
  53.1 8.2 %copy-start.4 = (f32[4,24,34,1]{3,2,1,0:T(8,128)S(1)}, f32[4,24,34,1]{3,2,1,0:T(8,128)}, u32[]{:S(2)}) copy-start(f32[4,24,34,1]{3,2,1,0:T(8,128)} %copy.24) | copy-start | bytes 39172
  53.1 8.2 %copy-start.6 = (f32[24,34,258]{2,1,0:T(8,128)S(1)}, f32[24,34,258]{2,1,0:T(8,128)}, u32[]{:S(2)}) copy-start(f32[24,34,258]{2,1,0:T(8,128)} %copy-done.5) | copy-start | bytes 2526340
  56.3 6.1 %copy-start.10 = (f32[24,34,258]{2,1,0:T(8,128)}, f32[24,34,258]{2,1,0:T(8,128)S(1)}, u32[]{:S(2)}) copy-start(f32[24,34,258]{2,1,0:T(8,128)S(1)} %compare_select_fusion) | copy-start | bytes 2526340
  56.3 5.1 %copy-start.3 = (f32[4,24,34,1]{3,2,1,0:T(8,128)S(1)}, f32[4,24,34,1]{3,2,1,0:T(8,128)}, u32[]{:S(2)}) copy-start(f32[4,24,34,1]{3,2,1,0:T(8,128)} %copy.22) | copy-start | bytes 39172
  61.3 1.1 copy-start.16
  62.5 1.0 copy-start.11
  63.5 2.9 copy-start.7
  69.5 0.8 slice-start.1
  70.3 15.7 %copy-start.20 = (f32[256]{0:T(256)S(1)}, f32[256]{0:T(256)}, u32[]{:S(2)}) copy-start(f32[256]{0:T(256)} %add_multiply_fusion) | copy-start | bytes 3076
  83.9 2.2 copy-start.12
  83.9 2.4 copy-start.14
  86.3 2.6 slice-start
  86.3 2.6 copy-start.15
  89.0 0.8 copy-start.17
  89.0 0.8 copy-start.21
  90.2 1.7 copy-start.8
  393.8 4.1 %copy-start.1 = (s32[128,2048]{1,0:T(8,128)S(1)}, s32[128,2048]{1,0:T(8,128)}, u32[]{:S(2)}) copy-start(s32[128,2048]{1,0:T(8,128)} %param.14) | copy-start | bytes 3145732
Sparse Core Ops, SparseCore 0:
  16.2 70.8 all-gather.2
  92.0 118.8 all-gather.4
where the time goes:
time: 408 us; the launch traced here: 405 us
  other arithmetic  177 us (43%)
  local copies, waits for them, and re-layouts  107 us (26%)
  waiting for transfers between devices  83.6 us (20%)
  between operations  13.8 us (3%)
  blocking collectives  13.5 us (3%)
  starting transfers between devices  8.1 us (2%)
    while x96, other arithmetic  118 us
    all_gather x1, waiting for transfers between devices, per_device(): lax.all_gather(forced, 'gz', axis=1, tiled=True)  82.5 us
    dynamic_update_slice x24, local copies, waits for them, and re-layouts, thomas(): lax.scan(forward, (ratio_start, zero_level), (rhs_lev, below_lev, above_l...  30.6 us
    concatenate x24, other arithmetic, thomas(): lax.scan(forward, (ratio_start, zero_level), (rhs_lev, below_lev, above_l...  25.3 us
    all_gather x1, blocking collectives, carried_in(): gathered = lax.all_gather(part, axis)  13.5 us
    slice x1, local copies, waits for them, and re-layouts, tridiagonal(): below[:, :-1]  13.2 us
    concatenate x1, local copies, waits for them, and re-layouts, tridiagonal(): jnp.concatenate([jnp.zeros_like(below[:, :1]), below[:, :-1]], axis=1)  12 us
    unnamed x45, local copies, waits for them, and re-layouts  9.96 us
  transfers between devices with their start and end apart: 6, of which 2 were waited for; matrix products, arithmetic and copies ran while one was open for 20% of the time, Pallas kernels for 0%

commit v1 on v0

--- a/solution.py
+++ b/solution.py
@@ -133,7 +133,9 @@
     forced = forced.at[2:].add(wind[:, None] * top_level[None, :, None, None] * wet_inner[None])
     coupling = mixing * (wet_inner * wet_next)[None]
     whole_forced, whole_coupling = (
-        lax.all_gather(forced, "gz", axis=1, tiled=True),
+        jnp.concatenate(
+            lax.all_to_all(jnp.stack([forced] * lax.axis_size("gz")), "gz", 0, 0), axis=1
+        ),
         lax.all_gather(coupling, "gz", axis=1, tiled=True),
     )
     solved = tridiagonal(whole_forced, whole_coupling)

time: 408 us -> 447 us (1.096)
  waiting for transfers between devices: 83.6 us -> 102 us
  other arithmetic: 177 us -> 184 us
  starting transfers between devices: 8.1 us -> 14.5 us
  local copies, waits for them, and re-layouts: 107 us -> 112 us
    all_to_all x0 -> x1, waiting for transfers between devices: none -> 102 us  [per_device(): lax.all_to_all(jnp.stack([forced] * lax.axis_size('gz')), 'gz', 0, 0)]
    all_gather x1 -> x0, waiting for transfers between devices: 82.5 us -> none  [per_device(): lax.all_gather(forced, 'gz', axis=1, tiled=True)]
    all_to_all x0 -> x1, starting transfers between devices: none -> 6.52 us  [per_device(): lax.all_to_all(jnp.stack([forced] * lax.axis_size('gz')), 'gz', 0, 0)]
    another operation x1 -> x2, local copies, waits for them, and re-layouts: 6.16 us -> 12.2 us
    unnamed x45 -> x29, local copies, waits for them, and re-layouts: 9.96 us -> 12.2 us
  transfers between devices with their start and end apart: 6 -> 6, of which waited for: 2 -> 1; matrix products, arithmetic and copies ran while one was open for 20% -> 23% of each run, Pallas kernels for 0% -> 0%
where the time goes in v1:
time: 447 us; the launch traced here: 441 us
  other arithmetic  184 us (41%)
  local copies, waits for them, and re-layouts  112 us (25%)
  waiting for transfers between devices  102 us (23%)
  starting transfers between devices  14.5 us (3%)
  between operations  13.8 us (3%)
  blocking collectives  13.4 us (3%)
    while x96, other arithmetic  118 us
    all_to_all x1, waiting for transfers between devices, per_device(): lax.all_to_all(jnp.stack([forced] * lax.axis_size('gz')), 'gz', 0, 0)  102 us
    dynamic_update_slice x24, local copies, waits for them, and re-layouts, thomas(): lax.scan(forward, (ratio_start, zero_level), (rhs_lev, below_lev, above_l...  31.5 us
    concatenate x24, other arithmetic, thomas(): lax.scan(forward, (ratio_start, zero_level), (rhs_lev, below_lev, above_l...  25.3 us
    all_gather x1, blocking collectives, carried_in(): gathered = lax.all_gather(part, axis)  13.4 us
    unnamed x29, local copies, waits for them, and re-layouts  12.2 us
    concatenate x1, local copies, waits for them, and re-layouts, tridiagonal(): jnp.concatenate([jnp.zeros_like(below[:, :1]), below[:, :-1]], axis=1)  11.8 us
    slice x1, local copies, waits for them, and re-layouts, tridiagonal(): below[:, :-1]  11.7 us
  transfers between devices with their start and end apart: 6, of which 1 were waited for; matrix products, arithmetic and copies ran while one was open for 23% of the time, Pallas kernels for 0%

profile of v1, /device:TPU:1, one launch (start us, length us, event | category | flops | bytes accessed | tf_op | source)
XLA Modules:
  0.0 441.1 jit_solution(5483393616034429387)
XLA Ops:
  8.1 2.7 collective-permute-start
  15.1 2.8 broadcast_multiply_fusion
  18.0 4.0 constant_dynamic-update-slice_fusion
  22.0 2.5 pad_maximum_fusion.7
  24.5 2.6 fusion.103
  27.1 2.3 copy.21
  29.4 2.5 collective-permute-start.2
  31.9 2.4 copy.23
  34.3 2.8 collective-permute-start.3
  37.1 2.8 dynamic-update-slice.30
  39.9 2.2 broadcast_maximum_fusion.1
  44.1 2.9 multiply_subtract_fusion.1
  47.8 2.1 copy.24
  49.9 3.2 compare_select_fusion
  54.2 5.0 %fusion.106 = f32[24,34,258]{2,1,0:T(8,128)S(1)} fusion(f32[24,34,258]{2,1,0:T(8,128)S(1)} %compare_select_fusion), kind=kOutput, calls=%fused_computation.238 | output fusion | flops 4842144 | bytes 1684224 | tf_op jit(solution)/shard_map/jit(cumsum)/reduce_window_sum | solution.py:120
  60.3 13.4 %all_gather.7 = f32[4,34,258]{2,1,0:T(8,128)S(1)} all-gather(f32[1,34,258]{2,1,0:T(8,128)S(1)} %slice.516), channel_id=1, replica_groups=mesh['gx'=4,'gy'=8,'gz'=4] {'gz'}, dimensions={0}, use_global_device_ids=true | all-gather | bytes 175440 | tf_op jit(solution)/shard_map/all_gather | solution.py:22
  73.8 2.2 subtract_multiply_fusion
  76.2 3.2 broadcast_maximum_fusion
  81.7 4.2 multiply_subtract_fusion
  85.9 6.6 %fusion.43 = f32[4,24,32,256]{3,2,1,0:T(8,128)} fusion(f32[4,24,32,256]{3,2,1,0:T(8,128)S(1)} %copy-done.3, f32[4,24,32,257]{3,2,1,0:T(8,128)} %multiply_subtract_fusion, f32[4,24,33,256]{3,2,1,0:T(8,128)S(1)} %copy-done.6), kind=kLoop, calls=%fused_computation.135 | loop fusion | flops 3145728 | bytes 18874368 | tf_op jit(solution)/shard_map/sub | solution.py:51
  93.8 2.6 fusion.69
  98.0 6.1 %stack.20 = f32[4,4,24,32,256]{4,3,1,2,0:T(8,128)} broadcast(f32[4,24,32,256]{3,2,0,1:T(8,128)S(1)} %copy.27), dimensions={1,2,3,4} | broadcast | bytes 15728640 | tf_op jit(solution)/shard_map/stack | solution.py:137
  104.1 6.5 %all-to-all-start = ((f32[4,4,24,32,256]{4,3,1,2,0:T(8,128)}), f32[4,4,24,32,256]{4,3,1,2,0:T(8,128)}, u32[]{:S(2)}, u32[]{:S(2)}) async-start(f32[4,4,24,32,256]{4,3,1,2,0:T(8,128)} %stack.20), calls=%async_computation | async-start | bytes 25165824 | tf_op jit(solution)/shard_map/all_to_all | solution.py:137
  110.7 3.9 copy.20
  114.6 6.7 %broadcast_in_dim.186 = f32[2,2,96,32,256]{4,3,1,0,2:T(8,128)} broadcast(f32[2,96,32,256]{3,2,0,1:T(8,128)S(1)} %copy.20), dimensions={0,2,3,4} | broadcast | bytes 18874368 | tf_op jit(solution)/shard_map/broadcast_in_dim | solution.py:95
  121.3 11.7 %slice.499 = f32[4,95,32,256]{3,2,0,1:T(8,128)} slice(f32[4,96,32,256]{3,2,0,1:T(8,128)} %bitcast.472), slice={[0:4], [0:95], [0:32], [0:256]} | slice | bytes 24903680 | tf_op jit(solution)/shard_map/slice | solution.py:96
  133.1 11.8 %concatenate.46 = f32[4,96,32,256]{3,2,0,1:T(8,128)} pad(f32[4,95,32,256]{3,2,0,1:T(8,128)} %slice.499, f32[]{:T(128)} %constant.188.clone.1), padding=0_0x1_0x0_0x0_0 | pad | bytes 25034756 | tf_op jit(solution)/shard_map/concatenate | solution.py:96
  144.9 101.6 %all-to-all-done = f32[4,4,24,32,256]{4,3,1,2,0:T(8,128)} async-done(((f32[4,4,24,32,256]{4,3,1,2,0:T(8,128)}), f32[4,4,24,32,256]{4,3,1,2,0:T(8,128)}, u32[]{:S(2)}, u32[]{:S(2)}) %all-to-all-start) | async-done | bytes 12582944 | tf_op jit(solution)/shard_map/all_to_all | solution.py:137
  246.5 141.6 %while.46 = (s32[]{:T(128)}, f32[4,32,256]{2,1,0:T(8,128)S(1)}, f32[4,32,256]{2,1,0:T(8,128)S(1)}, f32[12,8,4,32,256]{4,3,2,1,0:T(8,128)}, f32[12,8,4,32,256]{4,...) while((s32[]{:T(128)}, f32[4,32,256]{2,1,0:T(8,128)S(1)}, ...), condition=%wide.region_4.5_spmd.clone, body=%wide.region_3.4_spmd.clone.sunk | while | flops 2162696 | bytes 14943063 | solution.py:81
  388.1 6.1 %broadcast.318.clone = f32[12,8,4,32,256]{4,3,1,0,2:T(8,128)} broadcast(f32[]{:T(128)} %constant.188.clone.1), dimensions={} | broadcast | bytes 12582916 | tf_op jit(solution)/shard_map/broadcast.15
  394.2 36.0 %while.47 = (s32[]{:T(128)}, f32[4,32,256]{2,1,0:T(8,128)S(1)}, f32[12,8,4,32,256]{4,3,1,0,2:T(8,128)}, f32[12,8,4,32,256]{4,3,2,1,0:T(8,128)}, f32[12,8,4,32,25...) while((s32[]{:T(128)}, f32[4,32,256]{2,1,0:T(8,128)S(1)}, ...), condition=%wide.region_6.7_spmd.clone, body=%wide.region_5.6_spmd.clone.sunk | while | flops 557066 | bytes 7340315 | solution.py:90
  430.2 4.1 dynamic-slice_bitcast_fusion.40
  (302 shorter events, 192.6 us)
Async XLA Ops:
  6.5 4.4 copy-start
  6.5 104.2 %all-gather.2.cloned.1.call-start = ((), (), s32[]{:S(2)}) async-start(), calls=%async_computation.1 | async-start | bytes 7864320 | tf_op jit(solution)/shard_map/all_gather | solution.py:139
  8.1 13.9 %collective-permute-start = (f32[4,24,1,256]{3,2,1,0:T(1,128)S(1)}, f32[4,24,1,256]{3,2,1,0:T(1,128)S(1)}, u32[]{:S(2)}, u32[]{:S(2)}) collective-permute-start(f32[4,24,1,256]{3,2,1,0:T(1,128)S(1)} %get-tuple-element.323), channel_id=1, source_target_pairs={{0,32},{32,64},{64,96},{96,0},{1,33},{33,65},{65,97},{97,1},{2,34}... | collective-permute-start | bytes 294920 | tf_op jit(solution)/shard_map/ppermute | solution.py:14
  10.8 11.2 %collective-permute-start.1 = (f32[4,24,1,256]{3,2,1,0:T(1,128)S(1)}, f32[4,24,1,256]{3,2,1,0:T(1,128)S(1)}, u32[]{:S(2)}, u32[]{:S(2)}) collective-permute-start(f32[4,24,1,256]{3,2,1,0:T(1,128)S(1)} %get-tuple-element.324), channel_id=1, source_target_pairs={{32,0},{64,32},{96,64},{0,96},{33,1},{65,33},{97,65},{1,97},{34,2}... | collective-permute-start | bytes 294920 | tf_op jit(solution)/shard_map/ppermute | solution.py:15
  13.7 26.2 %copy-start.5 = (f32[24,34,258]{2,1,0:T(8,128)}, f32[24,34,258]{2,1,0:T(8,128)S(1)}, u32[]{:S(2)}) copy-start(f32[24,34,258]{2,1,0:T(8,128)S(1)} %compare_convert_fusion) | copy-start | bytes 2526340
  29.4 17.6 %collective-permute-start.2 = (f32[4,24,34,1]{2,1,3,0:T(8,128)S(1)}, f32[4,24,34,1]{2,1,3,0:T(8,128)S(1)}, u32[]{:S(2)}, u32[]{:S(2)}) collective-permute-start(f32[4,24,34,1]{2,1,3,0:T(8,128)S(1)} %copy.21), channel_id=1, source_target_pairs={{0,4},{4,8},{8,12},{12,16},{16,20},{20,24},{24,28},{28,0},{1,5},{5... | collective-permute-start | bytes 39176 | tf_op jit(solution)/shard_map/ppermute | solution.py:14
  34.3 13.5 %collective-permute-start.3 = (f32[4,24,34,1]{2,1,3,0:T(8,128)S(1)}, f32[4,24,34,1]{2,1,3,0:T(8,128)S(1)}, u32[]{:S(2)}, u32[]{:S(2)}) collective-permute-start(f32[4,24,34,1]{2,1,3,0:T(8,128)S(1)} %copy.23), channel_id=1, source_target_pairs={{4,0},{8,4},{12,8},{16,12},{20,16},{24,20},{28,24},{0,28},{5,1},{9... | collective-permute-start | bytes 39176 | tf_op jit(solution)/shard_map/ppermute | solution.py:15
  39.9 2.8 copy-start.7
  42.1 2.0 copy-start.2
  53.1 1.1 copy-start.8
  59.1 1.1 copy-start.12
  73.8 2.4 copy-start.4
  79.4 1.0 copy-start.9
  79.4 2.3 copy-start.3
  81.7 4.2 copy-start.6
  92.5 1.3 copy-start.10
  93.8 2.6 slice-start
  93.8 2.6 copy-start.11
  96.4 0.8 copy-start.13
  104.1 142.4 %all-to-all-start = ((f32[4,4,24,32,256]{4,3,1,2,0:T(8,128)}), f32[4,4,24,32,256]{4,3,1,2,0:T(8,128)}, u32[]{:S(2)}, u32[]{:S(2)}) async-start(f32[4,4,24,32,256]{4,3,1,2,0:T(8,128)} %stack.20), calls=%async_computation | async-start | bytes 25165824 | tf_op jit(solution)/shard_map/all_to_all | solution.py:137
  430.2 4.1 copy-start.1
Sparse Core Ops, SparseCore 0:
  18.1 70.0 all-gather.1
